TPU v7x, 32 devices: a whole 2x2x4 slice. The times are simulated.
32 devices in a mesh: row: 4 (over z), col: 8 (over y, x, core).
Axes of the slice: x: 2, y: 2, z: 4, core: 2. Of those that a mesh axis runs over, the one named last changes fastest.
Arguments:
- xn: bfloat16 [256, 2048], P('col', 'row'), may hold values from -6 to 6
- w_qkv: bfloat16 [2048, 6144], P('row', 'col'), may hold values from -0.125 to 0.125
- w_out: bfloat16 [2048, 2048], P('col', 'row'), may hold values from -0.125 to 0.125
- pool: bfloat16 [1024, 64, 4096], P('row', None, 'col'), may hold values from -136 to 136
- page_table: int32 [256, 64], P('row'), may hold values from 0 to 271
- lengths: int32 [256], P('row'), may hold values from 1 to 4096, 24576 in all
- mig_src: int32 [64], replicated, may hold values from 0 to 1023, as said below
- deal: int32 [256], replicated, may hold values from 0 to 255, each once
Outputs:
- attended: bfloat16 [256, 2048], P('col', 'row')
- landed: bfloat16 [64, 64, 4096], P('row', None, 'col')
Inputs may be any that keep to these rules, and one draw needn't show every extreme that they name: `page_table`: page ids of a request refer to its own row block: below 256 its pool pages, from 256 its landing slots. `lengths`: the longest request has exactly 4096 cache tokens. `mig_src`: slot d belongs to row block d // 16; its source page lies in the pool pages of another row block. `deal`: a permutation of the requests.
All inputs are finite; a program needn't handle non-finite values. No bound on the sum of `lengths` on one device may be relied on, other than what follows from the above.
Results may differ from a plain program's by a relative error of at most 0.02.
Values may be sent and summed in bfloat16 or wider, within the bound.
No kernel may reach another device: no remote copies, remote signals or barrier semaphores. Data moves between devices by JAX's collectives and lax.ppermute only.
A program may use at most 128 MiB of HBM per device.

v0:
```python
import functools

import jax
import jax.numpy as jnp
from jax import lax
from jax.experimental import pallas as pl
from jax.experimental.pallas import tpu as pltpu
from jax.sharding import PartitionSpec as P

HEAD_DIM = 64
PAGE = 64


theta_base = 130000.0
neg_large = -1e30


def rotate(values, positions):
    half = values.shape[-1] // 2
    freqs = theta_base ** (-(jnp.arange(half, dtype=jnp.float32) * 2.0 / values.shape[-1]))
    angles = positions.astype(jnp.float32)[:, None, None] * freqs[None, None, :]
    cosine = jnp.cos(angles)
    sine = jnp.sin(angles)
    first = values[..., :half]
    second = values[..., half:]
    return jnp.concatenate(
        [first * cosine - second * sine, second * cosine + first * sine], axis=-1
    )


def page_scores(page_of, flat, scores, qrow, start, count, length, maxp):
    rows = qrow.shape[0]
    pos = lax.broadcasted_iota(jnp.int32, (rows, PAGE), 1)

    def one(k):
        j = flat[start + k] % maxp
        s = lax.dot_general(
            qrow, page_of(start + k), (((1,), (1,)), ((), ())),
            preferred_element_type=jnp.float32,
        ) * 0.125
        s = jnp.where(j * PAGE + pos < length, s, neg_large)
        scores[k] = s
        return s

    def two(k2, top):
        s0 = one(2 * k2)
        s1 = one(2 * k2 + 1)
        return jnp.maximum(top, jnp.maximum(s0, s1))

    top = lax.fori_loop(0, count // 2, two, jnp.full((rows, PAGE), neg_large, jnp.float32))
    top = lax.fori_loop(count // 2 * 2, count, lambda k, t: jnp.maximum(t, one(k)), top)
    return jnp.max(top, axis=1, keepdims=True)


def page_values(page_of, flat, scores, top, start, count, length, maxp, lanes):
    rows = top.shape[0]
    pos = lax.broadcasted_iota(jnp.int32, (rows, PAGE), 1)

    def one(k):
        j = flat[start + k] % maxp
        e = jnp.where(j * PAGE + pos < length, jnp.exp(scores[k] - top), 0.0)
        w = e.astype(jnp.bfloat16)
        return e, jnp.dot(w, page_of(start + k), preferred_element_type=jnp.float32)

    def two(k2, carry):
        total, numer = carry
        e0, n0 = one(2 * k2)
        e1, n1 = one(2 * k2 + 1)
        return total + (e0 + e1), numer + (n0 + n1)

    def single(k, carry):
        total, numer = carry
        e0, n0 = one(k)
        return total + e0, numer + n0

    init = (jnp.zeros((rows, PAGE), jnp.float32), jnp.zeros((rows, lanes), jnp.float32))
    carry = lax.fori_loop(0, count // 2, two, init)
    total, numer = lax.fori_loop(count // 2 * 2, count, single, carry)
    return jnp.sum(total, axis=1, keepdims=True), numer


def build_list(tbl, lens, pool_n, maxp, reqs, flat, starts, listed, landing):
    def req(r, carry):
        n, nl = carry
        starts[r] = n
        count = (lens[r] + PAGE - 1) // PAGE

        def page(j, n):
            e = r * maxp + j
            flat[n] = e
            keep = (tbl[e] >= pool_n) if landing else (tbl[e] < pool_n)
            return n + keep.astype(jnp.int32)

        n2 = lax.fori_loop(0, count, page, n)
        listed[nl] = r
        return n2, nl + (n2 > n).astype(jnp.int32)

    n, nl = lax.fori_loop(0, reqs, req, (0, 0))
    starts[reqs] = n
    return n, nl


def query_rows(qwide_ref, r, rows):
    lanes = qwide_ref.shape[2]
    wide = jnp.broadcast_to(qwide_ref[r], (rows, lanes))
    head = lax.broadcasted_iota(jnp.int32, (rows, lanes), 0)
    lane = lax.broadcasted_iota(jnp.int32, (rows, lanes), 1)
    return jnp.where(head == lane // 128, wide, 0.0).astype(jnp.bfloat16)


def pool_kernel(tbl, lens, qrow_ref, snew_ref, pool_ref,
                m_ref, l_ref, n_ref, scores, flat, starts, listed):
    reqs, rows, lanes = snew_ref.shape[0], snew_ref.shape[1], pool_ref.shape[2]
    maxp = scores.shape[0]
    pool_n = pool_ref.shape[0]
    build_list(tbl, lens, pool_n, maxp, reqs, flat, starts, listed, False)
    page_of = lambda f: pool_ref[jnp.clip(tbl[flat[f]], 0, pool_n - 1)]

    def request(r, carry):
        start = starts[r]
        count = starts[r + 1] - start
        length = lens[r]
        snew = snew_ref[r][:, :1]
        top = page_scores(page_of, flat, scores, query_rows(qrow_ref, r, rows), start, count,
                          length, maxp)
        top = jnp.maximum(top, snew)
        total, numer = page_values(page_of, flat, scores, top, start, count, length, maxp,
                                   lanes)
        m_ref[r] = jnp.broadcast_to(top, (rows, 128))
        l_ref[r] = jnp.broadcast_to(total, (rows, 128))
        n_ref[r] = numer
        return carry

    lax.fori_loop(0, reqs, request, 0)


def land_kernel(tbl, lens, qrow_ref, m_in, l_in, n_in, land_ref, pool_n_ref,
                m_ref, l_ref, n_ref, scores, flat, starts, listed):
    reqs, rows, lanes = m_in.shape[0], m_in.shape[1], land_ref.shape[2]
    maxp = scores.shape[0]
    pool_n = pool_n_ref.shape[0]
    land_n = land_ref.shape[0]
    _, listed_n = build_list(tbl, lens, pool_n, maxp, reqs, flat, starts, listed, True)
    m_ref[...] = m_in[...]
    l_ref[...] = l_in[...]
    n_ref[...] = n_in[...]
    page_of = lambda f: land_ref[jnp.clip(tbl[flat[f]] - pool_n, 0, land_n - 1)]

    def request(k, carry):
        r = listed[k]
        start = starts[r]
        count = starts[r + 1] - start
        length = lens[r]
        top_a = m_in[r][:, :1]
        top_b = page_scores(page_of, flat, scores, query_rows(qrow_ref, r, rows), start, count,
                            length, maxp)
        top = jnp.maximum(top_a, top_b)
        total, numer = page_values(page_of, flat, scores, top, start, count, length, maxp,
                                   lanes)
        scale = jnp.exp(top_a - top)
        m_ref[r] = jnp.broadcast_to(top, (rows, 128))
        l_ref[r] = jnp.broadcast_to(total + l_in[r][:, :1] * scale, (rows, 128))
        n_ref[r] = numer + n_in[r] * scale
        return carry

    lax.fori_loop(0, listed_n, request, 0)


def attend(qk, value_new, table, lens, pool, landed_fn):
    req_count = qk.shape[0]
    lanes = pool.shape[2]
    heads_here = lanes // (2 * HEAD_DIM)
    maxp = table.shape[1]
    pool_n = pool.shape[0]
    rows = 8
    lane = jnp.arange(lanes, dtype=jnp.int32)
    qwide = jnp.where((lane % 128 < HEAD_DIM)[None, :], qk.astype(jnp.float32), 0.0)
    qwide = qwide.reshape(req_count, 1, lanes)
    grouped = qk.astype(jnp.float32).reshape(req_count, heads_here, 2 * HEAD_DIM)
    score_new = jnp.sum(grouped[..., :HEAD_DIM] * grouped[..., HEAD_DIM:], axis=-1) * 0.125
    vf = value_new.astype(jnp.float32).reshape(req_count, heads_here, HEAD_DIM)
    snew = jnp.zeros((req_count, rows, 128), jnp.float32) + jnp.pad(
        score_new, ((0, 0), (0, rows - heads_here)))[:, :, None]
    tbl = table.reshape(-1)

    full = lambda shape: pl.BlockSpec(shape, lambda i, *_: (0,) * len(shape))
    big = (req_count, rows, lanes)
    small = (req_count, rows, 128)
    wide = (req_count, 1, lanes)
    scratch = [
        pltpu.VMEM((maxp, rows, PAGE), jnp.float32),
        pltpu.SMEM((req_count * maxp,), jnp.int32),
        pltpu.SMEM((req_count + 1,), jnp.int32),
        pltpu.SMEM((req_count,), jnp.int32),
    ]
    params = pltpu.CompilerParams(
        dimension_semantics=("arbitrary",), vmem_limit_bytes=60 * 1024 * 1024)
    state = [
        jax.ShapeDtypeStruct(small, jnp.float32),
        jax.ShapeDtypeStruct(small, jnp.float32),
        jax.ShapeDtypeStruct(big, jnp.float32),
    ]
    m_a, l_a, n_a = pl.pallas_call(
        pool_kernel,
        grid_spec=pltpu.PrefetchScalarGridSpec(
            num_scalar_prefetch=2,
            grid=(1,),
            in_specs=[full(wide), full(small), pl.BlockSpec(memory_space=pltpu.VMEM)],
            out_specs=[full(small), full(small), full(big)],
            scratch_shapes=scratch,
        ),
        out_shape=state,
        compiler_params=params,
    )(tbl, lens, qwide, snew, pool)

    landed = landed_fn(n_a)
    m_b, l_b, n_b = pl.pallas_call(
        land_kernel,
        grid_spec=pltpu.PrefetchScalarGridSpec(
            num_scalar_prefetch=2,
            grid=(1,),
            in_specs=[full(wide), full(small), full(small), full(big),
                      pl.BlockSpec(memory_space=pltpu.VMEM), pl.BlockSpec(memory_space=pl.ANY)],
            out_specs=[full(small), full(small), full(big)],
            scratch_shapes=scratch,
        ),
        out_shape=state,
        compiler_params=params,
    )(tbl, lens, qwide, m_a, l_a, n_a, landed, pool)
    top = m_b[:, :heads_here, :1]
    e_new = jnp.exp(score_new[:, :, None] - top)
    w_new = e_new.astype(jnp.bfloat16).astype(jnp.float32)
    numer = n_b[:, :heads_here].reshape(req_count, heads_here, heads_here, 2, HEAD_DIM)
    numer = jnp.stack([numer[:, h, h, 1] for h in range(heads_here)], axis=1)
    picked = ((numer + w_new * vf) / (l_b[:, :heads_here, :1] + e_new)).astype(jnp.bfloat16)
    return picked, landed


def migration_plan(pool, mig_src, row_count):
    pool_dev = pool.shape[0]
    land_all = mig_src.shape[0]
    land_dev = land_all // row_count
    src_row = jnp.clip(mig_src // pool_dev, 0, row_count - 1)
    local_page = jnp.clip(mig_src - src_row * pool_dev, 0, pool_dev - 1)
    dst_row = jnp.arange(land_all, dtype=jnp.int32) // land_dev
    onehot = (src_row[:, None] == jnp.arange(row_count, dtype=jnp.int32)[None, :]).astype(jnp.int32)
    csum = jnp.cumsum(onehot.reshape(row_count, land_dev, row_count), axis=1)
    csum = csum.reshape(land_all, row_count)
    rank = jnp.sum(csum * onehot, axis=1) - 1
    return dict(src_row=src_row, local_page=local_page, dst_row=dst_row, rank=rank,
                most=jnp.max(csum), land_dev=land_dev, first=max(1, (land_dev * 5 + 7) // 8))


def gather_kernel(idx_ref, pool_ref, out_ref, sems):
    count = out_ref.shape[0]
    pool_n = pool_ref.shape[0]

    def start(i, carry):
        src = jnp.clip(idx_ref[i], 0, pool_n - 1)
        pltpu.make_async_copy(pool_ref.at[src], out_ref.at[i], sems.at[i]).start()
        return carry

    def wait(i, carry):
        pltpu.make_async_copy(pool_ref.at[0], out_ref.at[i], sems.at[i]).wait()
        return carry

    lax.fori_loop(0, count, start, 0)
    lax.fori_loop(0, count, wait, 0)


def outgoing_pages(pool, plan, row_count, lo, size):
    my_row = lax.axis_index("row")
    rank = plan["rank"]
    sel = (plan["src_row"] == my_row) & (rank >= lo) & (rank < lo + size)
    where = jnp.where(sel, plan["dst_row"] * size + (rank - lo), row_count * size)
    idx = jnp.zeros((row_count * size,), jnp.int32).at[where].set(plan["local_page"], mode="drop")
    count = row_count * size
    pages = pl.pallas_call(
        gather_kernel,
        grid_spec=pltpu.PrefetchScalarGridSpec(
            num_scalar_prefetch=1,
            grid=(1,),
            in_specs=[pl.BlockSpec(memory_space=pl.ANY)],
            out_specs=pl.BlockSpec((count,) + pool.shape[1:], lambda i, *_: (0, 0, 0)),
            scratch_shapes=[pltpu.SemaphoreType.DMA((count,))],
        ),
        out_shape=jax.ShapeDtypeStruct((count,) + pool.shape[1:], pool.dtype),
        compiler_params=pltpu.CompilerParams(vmem_limit_bytes=32 * 1024 * 1024),
    )(idx, pool)
    return pages.reshape(row_count, size, pool.shape[1], pool.shape[2])


def migrate_first(pool, mig_src, row_count):
    plan = migration_plan(pool, mig_src, row_count)
    sent = outgoing_pages(pool, plan, row_count, 0, plan["first"])
    return lax.all_to_all(sent, "row", split_axis=0, concat_axis=0, tiled=True)


def migrate_rest(pool, mig_src, row_count, first_recv, dep):
    plan = migration_plan(pool, mig_src, row_count)
    land_dev, k1 = plan["land_dev"], plan["first"]
    my_row = lax.axis_index("row")
    mine = my_row * land_dev + jnp.arange(land_dev, dtype=jnp.int32)
    src_mine = plan["src_row"][mine]
    rank_mine = plan["rank"][mine]
    pool_dep, _ = lax.optimization_barrier((pool, dep))
    sizes = [0, land_dev - k1] if land_dev > k1 else [0]

    def branch(size):
        def run(pool_b, recv1):
            if size == 0:
                both = recv1
            else:
                sent = outgoing_pages(pool_b, plan, row_count, k1, size)
                recv2 = lax.all_to_all(sent, "row", split_axis=0, concat_axis=0, tiled=True)
                both = jnp.concatenate([recv1, recv2], axis=1)
            width = k1 + size
            flat = both.reshape(row_count * width, both.shape[2], both.shape[3])
            return jnp.take(flat, src_mine * width + jnp.clip(rank_mine, 0, width - 1), axis=0)
        return run

    need = jnp.maximum(plan["most"] - k1, 0)
    index = jnp.sum((jnp.array(sizes, jnp.int32) < need).astype(jnp.int32))
    return lax.switch(index, [branch(b) for b in sizes], pool_dep, first_recv)


def on_device(xn, w_qkv, w_out, pool, page_table, lengths, mig_src, deal):
    heads_here = w_out.shape[0] // HEAD_DIM
    rows_all = xn.shape[0] * lax.axis_size("col")
    row_count = lax.axis_size("row")
    req_row = rows_all // row_count
    inverse = jnp.zeros((rows_all,), jnp.int32).at[deal].set(jnp.arange(rows_all, dtype=jnp.int32))
    gathered = lax.all_gather(xn, "col", axis=0, tiled=True)
    chosen = inverse
    heads3 = w_qkv.reshape(w_qkv.shape[0], heads_here, 3, HEAD_DIM)
    w_perm = jnp.concatenate(
        [heads3[:, :, :2].reshape(w_qkv.shape[0], -1), heads3[:, :, 2].reshape(w_qkv.shape[0], -1)],
        axis=1)
    partial = jnp.dot(jnp.take(gathered, chosen, axis=0), w_perm,
                      preferred_element_type=jnp.float32).astype(jnp.bfloat16)
    parts = lax.all_to_all(partial, "row", split_axis=0, concat_axis=0, tiled=True)
    projected = jnp.sum(parts.reshape(row_count, req_row, -1).astype(jnp.float32), axis=0)
    qk_lanes = heads_here * 2 * HEAD_DIM
    x = projected[:, :qk_lanes]
    lane = jnp.arange(qk_lanes, dtype=jnp.int32)
    within = lane % HEAD_DIM
    half = HEAD_DIM // 2
    freqs = theta_base ** (-(jnp.arange(half, dtype=jnp.float32) * 2.0 / HEAD_DIM))
    angles = lengths.astype(jnp.float32)[:, None] * freqs[None, :]
    cosine = jnp.tile(jnp.cos(angles), (1, qk_lanes // half))
    sine = jnp.tile(jnp.sin(angles), (1, qk_lanes // half))
    ahead = jnp.roll(x, -half, axis=1)
    behind = jnp.roll(x, half, axis=1)
    rotated = jnp.where((within < half)[None, :], x * cosine - ahead * sine,
                        x * cosine + behind * sine)
    qk = rotated.astype(jnp.bfloat16)
    value_new = projected[:, qk_lanes:].astype(jnp.bfloat16)
    first = migrate_first(pool, mig_src, row_count)
    mixed, landed = attend(qk, value_new, page_table, lengths, pool,
                           lambda dep: migrate_rest(pool, mig_src, row_count, first, dep))
    mixed = mixed.reshape(req_row, heads_here * HEAD_DIM)
    mixed_all = lax.all_gather(mixed, "row", axis=0, tiled=True)
    chosen = deal
    col_count = lax.axis_size("col")
    partial = jnp.dot(
        jnp.take(mixed_all, chosen, axis=0), w_out, preferred_element_type=jnp.float32
    ).astype(jnp.bfloat16)
    parts = lax.all_to_all(partial, "col", split_axis=0, concat_axis=0, tiled=True)
    attended = jnp.sum(
        parts.reshape(col_count, rows_all // col_count, -1).astype(jnp.float32), axis=0
    ).astype(jnp.bfloat16)
    return (attended, landed)


def solution(mesh):
    placed = (
        P("col", "row"),
        P("row", "col"),
        P("col", "row"),
        P("row", None, "col"),
        P("row", None),
        P("row"),
        P(),
        P(),
    )
    return jax.shard_map(
        on_device,
        mesh=mesh,
        in_specs=placed,
        out_specs=(P("col", "row"), P("row", None, "col")),
        check_vma=False,
    )
```

profile of v0, /device:TPU:0, one launch (start us, length us, event | category | flops | bytes accessed | tf_op | source)
XLA Modules:
  0.0 153.3 jit_solution(1384670676587159336)
XLA Ops:
  0.7 0.7 compare_select_fusion.4
  1.4 1.4 scatter_custom_fusion.1
  2.8 1.4 copy.43
  4.3 10.8 %all_gather.6 = bf16[256,512]{1,0:T(8,128)(2,1)S(1)} all-gather(bf16[32,512]{1,0:T(8,128)(2,1)S(1)} %copy-done.4), channel_id=1, replica_groups=mesh['row'=4,'col'=8] {'col'}, dimensions={0}, use_global_device_ids=true | all-gather | bytes 294912 | tf_op jit(solution)/shard_map/all_gather | solution.py:333
  15.1 1.2 gather_fusion.2
  16.2 1.2 convolution_convert_fusion
  17.4 4.9 %all-to-all-start.1 = ((bf16[4,64,768]{2,1,0:T(8,128)(2,1)}), bf16[4,64,768]{2,1,0:T(8,128)(2,1)S(1)}, u32[]{:S(2)}, u32[]{:S(2)}) async-start(bf16[4,64,768]{2,1,0:T(8,128)(2,1)} %bitcast.6), calls=%async_computation.1 | async-start | bytes 786432 | tf_op jit(solution)/shard_map/all_to_all | solution.py:341
  22.5 0.7 select_reduce_fusion
  23.3 0.8 scatter_custom_fusion.2.idx_ref
  24.1 4.8 %shard_map.105 = bf16[40,64,512]{2,1,0:T(8,128)(2,1)} custom-call(s32[40]{0:T(128)S(1)} %scatter_custom_fusion.2.idx_ref, bf16[256,64,512]{2,1,0:T(8,128)(2,1)} %pool_n_ref.1), custom_call_target="tpu_custom_call" | custom-call | tf_op jit(solution)/shard_map/pallas_call | solution.py:278
  28.9 5.6 %all-to-all-done.1 = bf16[4,64,768]{2,1,0:T(8,128)(2,1)S(1)} async-done(((bf16[4,64,768]{2,1,0:T(8,128)(2,1)}), bf16[4,64,768]{2,1,0:T(8,128)(2,1)S(1)}, u32[]{:S(2)}, u32[]{:S(2)}) %all-to-all-start.1) | async-done | bytes 393248 | tf_op jit(solution)/shard_map/all_to_all | solution.py:341
  34.5 3.8 %all-to-all-start.2 = ((bf16[4,10,64,512]{3,2,1,0:T(8,128)(2,1)}), bf16[4,10,64,512]{3,2,1,0:T(8,128)(2,1)S(1)}, u32[]{:S(2)}, u32[]{:S(2)}) async-start(bf16[4,10,64,512]{3,2,1,0:T(8,128)(2,1)} %bitcast.10), calls=%async_computation.2 | async-start | bytes 5242880 | tf_op jit(solution)/shard_map/all_to_all | solution.py:296
  38.3 0.7 gather_fusion.4
  39.0 0.7 gather_fusion.3
  39.7 0.1 multiply_cosine_fusion
  39.8 0.7 tile.8
  40.5 1.7 %copy.44 = f32[64,512]{1,0:T(8,128)} copy(f32[64,512]{0,1:T(8,128)} %bitcast.39) | data formatting | bytes 262144 | tf_op jit(solution)/shard_map/tile | solution.py:350
  42.2 0.7 tile.20
  43.0 1.7 %copy.45 = f32[64,512]{1,0:T(8,128)} copy(f32[64,512]{0,1:T(8,128)} %bitcast.40) | data formatting | bytes 262144 | tf_op jit(solution)/shard_map/tile | solution.py:351
  44.7 0.7 reshape.199.tbl
  45.9 0.6 fusion.26
  47.5 1.1 broadcast_select_fusion.2
  48.7 0.7 reshape.202.qrow_ref
  49.4 0.2 fusion.7
  49.7 0.8 add.114.snew_ref
  50.5 60.3 %shard_map.104 = (f32[64,8,128]{2,1,0:T(8,128)}, f32[64,8,128]{2,1,0:T(8,128)}, f32[64,8,512]{2,1,0:T(8,128)}) custom-call(s32[4096]{0:T(1024)} %reshape.199.tbl, s32[64]{0:T(128)} %lens.3, f32[64,1,512]{2,1,0:T(1,128)} %reshape.202.qrow_ref, f32[64,8,128]{2,1,0:T(8,128)} %add.114.snew_ref, bf16[256,64,512]{2,1,0:T(8,128)(2,1)} %pool_n_ref.1), custom_call_target="tpu_custom_call" | custom-call | tf_op jit(solution)/shard_map/pallas_call | solution.py:203
  110.8 0.5 copy.52
  111.3 3.0 %conditional.1 = (bf16[16,64,512]{2,1,0:T(8,128)(2,1)S(1)}) conditional(s32[]{:T(128)} %clamp.7, (s32[16]{0:T(128)S(1)}, s32[16]{0:T(128)S(1)}, bf16[4,10,64,512]{3,2,1,0:T(8,128)(2,1)S(1)}) %tuple.15, (s32[16]{0:T(128)S(1)}, s32[16]{0:T(128)S(1)}, s32[64]{0:T(128)S(1)}, s32[64]{0:T(128)S(1)}, s32[64]{0:T(128)S(1)}, /*index=5*/s32[64]{0:T(128)S(1)}, ...), branch_computations={%region_8.9_spmd, %region_9.11_spmd} | conditional | flops 2623379 | bytes 17307152 | solution.py:324
  111.4 1.6 %gather_fusion = bf16[16,64,512]{2,1,0:T(8,128)(2,1)} fusion(bf16[40,64,512]{2,1,0:T(8,128)(2,1)S(1)} %bitcast.34, s32[1024]{0:T(1024)S(1)} %pad_clamp_fusion), kind=kCustom, calls=%fused_computation | custom fusion | bytes 2097216 | tf_op jit(solution)/shard_map/cond/branch_0_fun/jit(_take)/gather | solution.py:319
  113.0 1.4 broadcast_select_fusion
  114.4 10.2 %shard_map.106 = (f32[64,8,128]{2,1,0:T(8,128)}, f32[64,8,128]{2,1,0:T(8,128)}, f32[64,8,512]{2,1,0:T(8,128)}) custom-call(s32[4096]{0:T(1024)} %reshape.199.tbl, s32[64]{0:T(128)} %lens.3, f32[64,1,512]{2,1,0:T(1,128)} %reshape.202.qrow_ref, f32[64,8,128]{2,1,0:T(8,128)} %get-tuple-element.45.m_in, f32[64,8,128]{2,1,0:T(8,128)} %get-tuple-element.46.l_in, ...), custom_call_target="tpu_custom_call" | custom-call | tf_op jit(solution)/shard_map/pallas_call | solution.py:217
  124.6 1.4 slice.69
  125.9 0.8 reshape.205
  126.7 0.1 slice_bitcast_fusion.3
  126.9 0.2 pad_maximum_fusion.1
  127.0 0.1 stack.6
  127.3 0.1 copy.55
  127.4 0.1 copy.56
  127.5 0.1 div.52
  127.6 0.1 div.53
  127.8 0.1 copy.54
  127.9 0.1 mul.107
  128.1 0.1 mul.108
  128.3 13.4 %all_gather.7 = bf16[256,256]{1,0:T(8,128)(2,1)S(1)} all-gather(bf16[64,256]{1,0:T(8,128)(2,1)S(1)} %divide_convert_fusion), channel_id=1, replica_groups=mesh['row'=4,'col'=8] {'row'}, dimensions={0}, use_global_device_ids=true | all-gather | bytes 163840 | tf_op jit(solution)/shard_map/all_gather | solution.py:362
  141.7 1.2 gather_fusion.5
  142.8 0.3 convolution_convert_fusion.1
  143.1 9.5 %all_to_all.27 = bf16[8,32,512]{2,1,0:T(8,128)(2,1)S(1)} all-to-all(bf16[8,32,512]{2,1,0:T(8,128)(2,1)S(1)} %bitcast.38), channel_id=1, replica_groups=mesh['row'=4,'col'=8] {'col'}, dimensions={0} | all-to-all | bytes 524288 | tf_op jit(solution)/shard_map/all_to_all | solution.py:368
  152.6 0.7 reduce_sum.56
  (51 shorter events, 1.0 us)
Async XLA Ops:
  0.6 142.2 %copy-start = (bf16[256,512]{1,0:T(8,128)(2,1)S(1)}, bf16[256,512]{1,0:T(8,128)(2,1)}, u32[]{:S(2)}) copy-start(bf16[256,512]{1,0:T(8,128)(2,1)} %param.13) | copy-start | bytes 786436
  0.6 3.7 %copy-start.4 = (bf16[32,512]{1,0:T(8,128)(2,1)S(1)}, bf16[32,512]{1,0:T(8,128)(2,1)}, u32[]{:S(2)}) copy-start(bf16[32,512]{1,0:T(8,128)(2,1)} %param.11) | copy-start | bytes 98308
  15.1 7.2 %copy-start.8 = (s32[64]{0:T(128)S(1)}, s32[64]{0:T(128)}, u32[]{:S(2)}) copy-start(s32[64]{0:T(128)} %param.17) | copy-start | bytes 772
  17.4 17.1 %all-to-all-start.1 = ((bf16[4,64,768]{2,1,0:T(8,128)(2,1)}), bf16[4,64,768]{2,1,0:T(8,128)(2,1)S(1)}, u32[]{:S(2)}, u32[]{:S(2)}) async-start(bf16[4,64,768]{2,1,0:T(8,128)(2,1)} %bitcast.6), calls=%async_computation.1 | async-start | bytes 786432 | tf_op jit(solution)/shard_map/all_to_all | solution.py:341
  34.5 5.2 %copy-start.6 = (s32[64]{0:T(128)S(1)}, s32[64]{0:T(128)}, u32[]{:S(2)}) copy-start(s32[64]{0:T(128)} %lens.3) | copy-start | bytes 772
  34.5 10.2 %copy-start.5 = (s32[64,64]{1,0:T(8,128)S(1)}, s32[64,64]{1,0:T(8,128)}, u32[]{:S(2)}) copy-start(s32[64,64]{1,0:T(8,128)} %param.15) | copy-start | bytes 49156
  34.5 12.8 %copy-start.7 = (s32[256]{0:T(256)S(1)}, s32[256]{0:T(256)}, u32[]{:S(2)}) copy-start(s32[256]{0:T(256)} %param.18) | copy-start | bytes 3076
  34.5 76.9 %all-to-all-start.2 = ((bf16[4,10,64,512]{3,2,1,0:T(8,128)(2,1)}), bf16[4,10,64,512]{3,2,1,0:T(8,128)(2,1)S(1)}, u32[]{:S(2)}, u32[]{:S(2)}) async-start(bf16[4,10,64,512]{3,2,1,0:T(8,128)(2,1)} %bitcast.10), calls=%async_computation.2 | async-start | bytes 5242880 | tf_op jit(solution)/shard_map/all_to_all | solution.py:296
  114.4 10.2 %copy-start.1 = (bf16[16,64,512]{2,1,0:T(8,128)(2,1)}, bf16[16,64,512]{2,1,0:T(8,128)(2,1)S(1)}, u32[]{:S(2)}) copy-start(bf16[16,64,512]{2,1,0:T(8,128)(2,1)S(1)} %get-tuple-element.78.land_ref) | copy-start | bytes 3145732
  124.5 2.6 %copy-start.2 = (f32[64,8,128]{2,1,0:T(8,128)S(1)}, f32[64,8,128]{2,1,0:T(8,128)}, u32[]{:S(2)}) copy-start(f32[64,8,128]{2,1,0:T(8,128)} %get-tuple-element.50) | copy-start | bytes 786436
  124.6 2.6 %copy-start.3 = (f32[64,8,128]{2,1,0:T(8,128)S(1)}, f32[64,8,128]{2,1,0:T(8,128)}, u32[]{:S(2)}) copy-start(f32[64,8,128]{2,1,0:T(8,128)} %get-tuple-element.51) | copy-start | bytes 786436
where the time goes:
time: 151 us; the launch traced here: 153 us
  Pallas kernels  75.3 us (50%)
  blocking collectives  33.7 us (22%)
  local copies, waits for them, and re-layouts  20.3 us (13%)
  starting transfers between devices  8.65 us (6%)
  other arithmetic  6.14 us (4%)
  waiting for transfers between devices  5.58 us (4%)
  between operations  2.17 us (1%)
    pallas_call x1, Pallas kernels, attend(): pl.pallas_call(pool_kernel, grid_spec=pltpu.PrefetchScalarGridSpec(num_sc...  60.3 us
    all_gather x1, blocking collectives, on_device(): mixed_all = lax.all_gather(mixed, 'row', axis=0, tiled=True)  13.4 us
    all_gather x1, blocking collectives, on_device(): gathered = lax.all_gather(xn, 'col', axis=0, tiled=True)  10.8 us
    pallas_call x1, Pallas kernels, attend(): pl.pallas_call(land_kernel, grid_spec=pltpu.PrefetchScalarGridSpec(num_sc...  10.2 us
    all_to_all x1, blocking collectives, on_device(): lax.all_to_all(partial, 'col', split_axis=0, concat_axis=0, tiled=True)  9.5 us
    all_to_all x1, waiting for transfers between devices, on_device(): lax.all_to_all(partial, 'row', split_axis=0, concat_axis=0, tiled=True)  5.58 us
    all_to_all x1, starting transfers between devices, on_device(): lax.all_to_all(partial, 'row', split_axis=0, concat_axis=0, tiled=True)  4.87 us
    pallas_call x1, Pallas kernels, outgoing_pages(): pl.pallas_call(gather_kernel, grid_spec=pltpu.PrefetchScalarGridSpec(num_...  4.76 us
  transfers between devices with their start and end apart: 2, of which 1 were waited for; matrix products, arithmetic and copies ran while one was open for 9% of the time, Pallas kernels for 42%

commit v1 on v0

--- a/solution.py
+++ b/solution.py
@@ -135,32 +135,44 @@
 
 
 def land_kernel(tbl, lens, qrow_ref, m_in, l_in, n_in, land_ref, pool_n_ref,
-                m_ref, l_ref, n_ref, scores, flat, starts, listed):
+                m_ref, l_ref, n_ref, scores, flat, starts, listed, mbuf, lbuf, nbuf, sems):
     reqs, rows, lanes = m_in.shape[0], m_in.shape[1], land_ref.shape[2]
     maxp = scores.shape[0]
     pool_n = pool_n_ref.shape[0]
     land_n = land_ref.shape[0]
     _, listed_n = build_list(tbl, lens, pool_n, maxp, reqs, flat, starts, listed, True)
-    m_ref[...] = m_in[...]
-    l_ref[...] = l_in[...]
-    n_ref[...] = n_in[...]
     page_of = lambda f: land_ref[jnp.clip(tbl[flat[f]] - pool_n, 0, land_n - 1)]
+    pairs = ((m_in, m_ref, mbuf), (l_in, l_ref, lbuf), (n_in, n_ref, nbuf))
 
     def request(k, carry):
         r = listed[k]
+        reads = [pltpu.make_async_copy(src.at[pl.ds(r, 1)], buf, sems.at[i])
+                 for i, (src, _, buf) in enumerate(pairs)]
+        for c in reads:
+            c.start()
+        for c in reads:
+            c.wait()
         start = starts[r]
         count = starts[r + 1] - start
         length = lens[r]
-        top_a = m_in[r][:, :1]
+        top_a = mbuf[0][:, :1]
         top_b = page_scores(page_of, flat, scores, query_rows(qrow_ref, r, rows), start, count,
                             length, maxp)
         top = jnp.maximum(top_a, top_b)
         total, numer = page_values(page_of, flat, scores, top, start, count, length, maxp,
                                    lanes)
         scale = jnp.exp(top_a - top)
-        m_ref[r] = jnp.broadcast_to(top, (rows, 128))
-        l_ref[r] = jnp.broadcast_to(total + l_in[r][:, :1] * scale, (rows, 128))
-        n_ref[r] = numer + n_in[r] * scale
+        l_new = total + lbuf[0][:, :1] * scale
+        n_new = numer + nbuf[0] * scale
+        mbuf[0] = jnp.broadcast_to(top, (rows, 128))
+        lbuf[0] = jnp.broadcast_to(l_new, (rows, 128))
+        nbuf[0] = n_new
+        writes = [pltpu.make_async_copy(buf, dst.at[pl.ds(r, 1)], sems.at[i])
+                  for i, (_, dst, buf) in enumerate(pairs)]
+        for c in writes:
+            c.start()
+        for c in writes:
+            c.wait()
         return carry
 
     lax.fori_loop(0, listed_n, request, 0)
@@ -214,17 +226,24 @@
     )(tbl, lens, qwide, snew, pool)
 
     landed = landed_fn(n_a)
+    any_spec = pl.BlockSpec(memory_space=pl.ANY)
     m_b, l_b, n_b = pl.pallas_call(
         land_kernel,
         grid_spec=pltpu.PrefetchScalarGridSpec(
             num_scalar_prefetch=2,
             grid=(1,),
-            in_specs=[full(wide), full(small), full(small), full(big),
-                      pl.BlockSpec(memory_space=pltpu.VMEM), pl.BlockSpec(memory_space=pl.ANY)],
-            out_specs=[full(small), full(small), full(big)],
-            scratch_shapes=scratch,
+            in_specs=[full(wide), any_spec, any_spec, any_spec,
+                      pl.BlockSpec(memory_space=pltpu.VMEM), any_spec],
+            out_specs=[any_spec, any_spec, any_spec],
+            scratch_shapes=scratch + [
+                pltpu.VMEM((1, rows, 128), jnp.float32),
+                pltpu.VMEM((1, rows, 128), jnp.float32),
+                pltpu.VMEM((1, rows, lanes), jnp.float32),
+                pltpu.SemaphoreType.DMA((3,)),
+            ],
         ),
         out_shape=state,
+        input_output_aliases={3: 0, 4: 1, 5: 2},
         compiler_params=params,
     )(tbl, lens, qwide, m_a, l_a, n_a, landed, pool)
     top = m_b[:, :heads_here, :1]

time: 151 us -> 156 us (1.033)
  blocking collectives: 33.7 us -> 50.3 us
  Pallas kernels: 75.3 us -> 60.7 us
  waiting for transfers between devices: 5.58 us -> 8.38 us
    pallas_call x1, Pallas kernels: 60.3 us -> 43.1 us  [attend(): pl.pallas_call(pool_kernel, grid_spec=pltpu.PrefetchScalarGridSpec(num_sc...]
    all_gather x1, blocking collectives: 13.4 us -> 30.1 us  [on_device(): mixed_all = lax.all_gather(mixed, 'row', axis=0, tiled=True)]
    all_to_all x1, waiting for transfers between devices: 0.01 us -> 3.24 us  [migrate_first(): return lax.all_to_all(sent, 'row', split_axis=0, concat_axis=0, tiled=True)]
    pallas_call x1, Pallas kernels: 10.2 us -> 12.4 us  [attend(): pl.pallas_call(land_kernel, grid_spec=pltpu.PrefetchScalarGridSpec(num_sc...]
  transfers between devices with their start and end apart: 2 -> 2, of which waited for: 1 -> 2; matrix products, arithmetic and copies ran while one was open for 9% -> 8% of each run, Pallas kernels for 42% -> 31%
where the time goes in v1:
time: 156 us; the launch traced here: 158 us
  Pallas kernels  60.7 us (39%)
  blocking collectives  50.3 us (32%)
  local copies, waits for them, and re-layouts  20.3 us (13%)
  starting transfers between devices  8.65 us (6%)
  waiting for transfers between devices  8.38 us (5%)
  other arithmetic  6.13 us (4%)
  between operations  2.19 us (1%)
    pallas_call x1, Pallas kernels, attend(): pl.pallas_call(pool_kernel, grid_spec=pltpu.PrefetchScalarGridSpec(num_sc...  43.1 us
    all_gather x1, blocking collectives, on_device(): mixed_all = lax.all_gather(mixed, 'row', axis=0, tiled=True)  30.1 us
    pallas_call x1, Pallas kernels, attend(): pl.pallas_call(land_kernel, grid_spec=pltpu.PrefetchScalarGridSpec(num_sc...  12.4 us
    all_gather x1, blocking collectives, on_device(): gathered = lax.all_gather(xn, 'col', axis=0, tiled=True)  10.8 us
    all_to_all x1, blocking collectives, on_device(): lax.all_to_all(partial, 'col', split_axis=0, concat_axis=0, tiled=True)  9.5 us
    pallas_call x1, Pallas kernels, outgoing_pages(): pl.pallas_call(gather_kernel, grid_spec=pltpu.PrefetchScalarGridSpec(num_...  5.19 us
    all_to_all x1, waiting for transfers between devices, on_device(): lax.all_to_all(partial, 'row', split_axis=0, concat_axis=0, tiled=True)  5.15 us
    all_to_all x1, starting transfers between devices, on_device(): lax.all_to_all(partial, 'row', split_axis=0, concat_axis=0, tiled=True)  4.87 us
  transfers between devices with their start and end apart: 2, of which 2 were waited for; matrix products, arithmetic and copies ran while one was open for 8% of the time, Pallas kernels for 31%

profile of v1, /device:TPU:0, one launch (start us, length us, event | category | flops | bytes accessed | tf_op | source)
XLA Modules:
  0.0 158.2 jit_solution(5913636231760543546)
XLA Ops:
  0.7 0.7 compare_select_fusion.4
  1.4 1.4 scatter_custom_fusion.1
  2.8 1.4 copy.46
  4.3 10.8 %all_gather.6 = bf16[256,512]{1,0:T(8,128)(2,1)S(1)} all-gather(bf16[32,512]{1,0:T(8,128)(2,1)S(1)} %copy-done.4), channel_id=1, replica_groups=mesh['row'=4,'col'=8] {'col'}, dimensions={0}, use_global_device_ids=true | all-gather | bytes 294912 | tf_op jit(solution)/shard_map/all_gather | solution.py:352
  15.1 1.2 gather_fusion.2
  16.2 1.2 convolution_convert_fusion
  17.4 4.9 %all-to-all-start.1 = ((bf16[4,64,768]{2,1,0:T(8,128)(2,1)}), bf16[4,64,768]{2,1,0:T(8,128)(2,1)S(1)}, u32[]{:S(2)}, u32[]{:S(2)}) async-start(bf16[4,64,768]{2,1,0:T(8,128)(2,1)} %bitcast.6), calls=%async_computation.1 | async-start | bytes 786432 | tf_op jit(solution)/shard_map/all_to_all | solution.py:360
  22.5 0.7 select_reduce_fusion
  23.3 0.8 scatter_custom_fusion.2.idx_ref
  24.1 5.2 %shard_map.105 = bf16[40,64,512]{2,1,0:T(8,128)(2,1)} custom-call(s32[40]{0:T(128)S(1)} %scatter_custom_fusion.2.idx_ref, bf16[256,64,512]{2,1,0:T(8,128)(2,1)} %pool_n_ref.1), custom_call_target="tpu_custom_call" | custom-call | tf_op jit(solution)/shard_map/pallas_call | solution.py:297
  29.3 5.1 %all-to-all-done.1 = bf16[4,64,768]{2,1,0:T(8,128)(2,1)S(1)} async-done(((bf16[4,64,768]{2,1,0:T(8,128)(2,1)}), bf16[4,64,768]{2,1,0:T(8,128)(2,1)S(1)}, u32[]{:S(2)}, u32[]{:S(2)}) %all-to-all-start.1) | async-done | bytes 393248 | tf_op jit(solution)/shard_map/all_to_all | solution.py:360
  34.5 3.8 %all-to-all-start.2 = ((bf16[4,10,64,512]{3,2,1,0:T(8,128)(2,1)}), bf16[4,10,64,512]{3,2,1,0:T(8,128)(2,1)S(1)}, u32[]{:S(2)}, u32[]{:S(2)}) async-start(bf16[4,10,64,512]{3,2,1,0:T(8,128)(2,1)} %bitcast.10), calls=%async_computation.2 | async-start | bytes 5242880 | tf_op jit(solution)/shard_map/all_to_all | solution.py:315
  38.3 0.7 gather_fusion.4
  39.0 0.7 gather_fusion.3
  39.7 0.1 multiply_cosine_fusion
  39.8 0.7 tile.8
  40.5 1.7 %copy.47 = f32[64,512]{1,0:T(8,128)} copy(f32[64,512]{0,1:T(8,128)} %bitcast.39) | data formatting | bytes 262144 | tf_op jit(solution)/shard_map/tile | solution.py:369
  42.2 0.7 tile.20
  43.0 1.7 %copy.48 = f32[64,512]{1,0:T(8,128)} copy(f32[64,512]{0,1:T(8,128)} %bitcast.40) | data formatting | bytes 262144 | tf_op jit(solution)/shard_map/tile | solution.py:370
  44.7 0.7 reshape.199.tbl
  45.9 0.6 fusion.26
  47.5 1.1 broadcast_select_fusion.2
  48.7 0.7 reshape.202.qrow_ref
  49.4 0.2 fusion.7
  49.7 0.8 add.114.snew_ref
  50.5 43.1 %shard_map.104 = (f32[64,8,128]{2,1,0:T(8,128)}, f32[64,8,128]{2,1,0:T(8,128)}, f32[64,8,512]{2,1,0:T(8,128)}) custom-call(s32[4096]{0:T(1024)} %reshape.199.tbl, s32[64]{0:T(128)} %lens.3, f32[64,1,512]{2,1,0:T(1,128)} %reshape.202.qrow_ref, f32[64,8,128]{2,1,0:T(8,128)} %add.114.snew_ref, bf16[256,64,512]{2,1,0:T(8,128)(2,1)} %pool_n_ref.1), custom_call_target="tpu_custom_call" | custom-call | tf_op jit(solution)/shard_map/pallas_call | solution.py:215
  93.6 0.5 copy.55
  94.1 3.2 %all-to-all-done.2 = bf16[4,10,64,512]{3,2,1,0:T(8,128)(2,1)S(1)} async-done(((bf16[4,10,64,512]{3,2,1,0:T(8,128)(2,1)}), bf16[4,10,64,512]{3,2,1,0:T(8,128)(2,1)S(1)}, u32[]{:S(2)}, u32[]{:S(2)}) %all-to-all-start.2) | async-done | bytes 2621472 | tf_op jit(solution)/shard_map/all_to_all | solution.py:315
  97.3 3.0 %conditional.1 = (bf16[16,64,512]{2,1,0:T(8,128)(2,1)S(1)}) conditional(s32[]{:T(128)} %clamp.7, (s32[16]{0:T(128)S(1)}, s32[16]{0:T(128)S(1)}, bf16[4,10,64,512]{3,2,1,0:T(8,128)(2,1)S(1)}) %tuple.15, (s32[16]{0:T(128)S(1)}, s32[16]{0:T(128)S(1)}, s32[64]{0:T(128)S(1)}, s32[64]{0:T(128)S(1)}, s32[64]{0:T(128)S(1)}, /*index=5*/s32[64]{0:T(128)S(1)}, ...), branch_computations={%region_8.9_spmd, %region_9.11_spmd} | conditional | flops 2623379 | bytes 17307152 | solution.py:343
  97.4 1.6 %gather_fusion = bf16[16,64,512]{2,1,0:T(8,128)(2,1)} fusion(bf16[40,64,512]{2,1,0:T(8,128)(2,1)S(1)} %bitcast.34, s32[1024]{0:T(1024)S(1)} %pad_clamp_fusion), kind=kCustom, calls=%fused_computation | custom fusion | bytes 2097216 | tf_op jit(solution)/shard_map/cond/branch_0_fun/jit(_take)/gather | solution.py:338
  99.0 1.4 broadcast_select_fusion
  100.4 12.4 %shard_map.106 = (f32[64,8,128]{2,1,0:T(8,128)}, f32[64,8,128]{2,1,0:T(8,128)}, f32[64,8,512]{2,1,0:T(8,128)}) custom-call(s32[4096]{0:T(1024)} %reshape.199.tbl, s32[64]{0:T(128)} %lens.3, f32[64,1,512]{2,1,0:T(1,128)} %reshape.202.qrow_ref, f32[64,8,128]{2,1,0:T(8,128)} %get-tuple-element.45.m_in, ...), custom_call_target="tpu_custom_call", output_to_operand_aliasing={{0}: (3, {}), {1}: (4, {}), {2}: (5, {})} | custom-call | tf_op jit(solution)/shard_map/pallas_call | solution.py:230
  112.8 1.3 slice.69
  114.2 0.8 reshape.205
  115.0 0.1 slice_bitcast_fusion.3
  115.2 0.2 pad_maximum_fusion.1
  115.3 0.1 stack.6
  115.6 0.1 copy.59
  115.7 0.1 div.52
  115.9 0.1 div.53
  116.1 0.1 copy.57
  116.2 0.1 mul.107
  116.4 0.1 mul.108
  116.5 30.1 %all_gather.7 = bf16[256,256]{1,0:T(8,128)(2,1)S(1)} all-gather(bf16[64,256]{1,0:T(8,128)(2,1)S(1)} %divide_convert_fusion), channel_id=1, replica_groups=mesh['row'=4,'col'=8] {'row'}, dimensions={0}, use_global_device_ids=true | all-gather | bytes 163840 | tf_op jit(solution)/shard_map/all_gather | solution.py:381
  146.6 1.2 gather_fusion.5
  147.8 0.3 convolution_convert_fusion.1
  148.0 9.5 %all_to_all.27 = bf16[8,32,512]{2,1,0:T(8,128)(2,1)S(1)} all-to-all(bf16[8,32,512]{2,1,0:T(8,128)(2,1)S(1)} %bitcast.38), channel_id=1, replica_groups=mesh['row'=4,'col'=8] {'col'}, dimensions={0} | all-to-all | bytes 524288 | tf_op jit(solution)/shard_map/all_to_all | solution.py:387
  157.5 0.7 reduce_sum.56
  (51 shorter events, 1.1 us)
Async XLA Ops:
  0.6 147.1 %copy-start = (bf16[256,512]{1,0:T(8,128)(2,1)S(1)}, bf16[256,512]{1,0:T(8,128)(2,1)}, u32[]{:S(2)}) copy-start(bf16[256,512]{1,0:T(8,128)(2,1)} %param.13) | copy-start | bytes 786436
  0.6 3.7 %copy-start.4 = (bf16[32,512]{1,0:T(8,128)(2,1)S(1)}, bf16[32,512]{1,0:T(8,128)(2,1)}, u32[]{:S(2)}) copy-start(bf16[32,512]{1,0:T(8,128)(2,1)} %param.11) | copy-start | bytes 98308
  15.1 7.2 %copy-start.8 = (s32[64]{0:T(128)S(1)}, s32[64]{0:T(128)}, u32[]{:S(2)}) copy-start(s32[64]{0:T(128)} %param.17) | copy-start | bytes 772
  17.4 17.1 %all-to-all-start.1 = ((bf16[4,64,768]{2,1,0:T(8,128)(2,1)}), bf16[4,64,768]{2,1,0:T(8,128)(2,1)S(1)}, u32[]{:S(2)}, u32[]{:S(2)}) async-start(bf16[4,64,768]{2,1,0:T(8,128)(2,1)} %bitcast.6), calls=%async_computation.1 | async-start | bytes 786432 | tf_op jit(solution)/shard_map/all_to_all | solution.py:360
  34.5 5.2 %copy-start.6 = (s32[64]{0:T(128)S(1)}, s32[64]{0:T(128)}, u32[]{:S(2)}) copy-start(s32[64]{0:T(128)} %lens.3) | copy-start | bytes 772
  34.5 10.2 %copy-start.5 = (s32[64,64]{1,0:T(8,128)S(1)}, s32[64,64]{1,0:T(8,128)}, u32[]{:S(2)}) copy-start(s32[64,64]{1,0:T(8,128)} %param.15) | copy-start | bytes 49156
  34.5 12.8 %copy-start.7 = (s32[256]{0:T(256)S(1)}, s32[256]{0:T(256)}, u32[]{:S(2)}) copy-start(s32[256]{0:T(256)} %param.18) | copy-start | bytes 3076
  34.5 62.9 %all-to-all-start.2 = ((bf16[4,10,64,512]{3,2,1,0:T(8,128)(2,1)}), bf16[4,10,64,512]{3,2,1,0:T(8,128)(2,1)S(1)}, u32[]{:S(2)}, u32[]{:S(2)}) async-start(bf16[4,10,64,512]{3,2,1,0:T(8,128)(2,1)} %bitcast.10), calls=%async_computation.2 | async-start | bytes 5242880 | tf_op jit(solution)/shard_map/all_to_all | solution.py:315
  100.4 12.5 %copy-start.1 = (bf16[16,64,512]{2,1,0:T(8,128)(2,1)}, bf16[16,64,512]{2,1,0:T(8,128)(2,1)S(1)}, u32[]{:S(2)}) copy-start(bf16[16,64,512]{2,1,0:T(8,128)(2,1)S(1)} %get-tuple-element.78.land_ref) | copy-start | bytes 3145732
  112.8 2.6 %copy-start.2 = (f32[64,8,128]{2,1,0:T(8,128)S(1)}, f32[64,8,128]{2,1,0:T(8,128)}, u32[]{:S(2)}) copy-start(f32[64,8,128]{2,1,0:T(8,128)} %get-tuple-element.50) | copy-start | bytes 786436
  112.8 2.6 %copy-start.3 = (f32[64,8,128]{2,1,0:T(8,128)S(1)}, f32[64,8,128]{2,1,0:T(8,128)}, u32[]{:S(2)}) copy-start(f32[64,8,128]{2,1,0:T(8,128)} %get-tuple-element.51) | copy-start | bytes 786436

commit v2 on v0

--- a/solution.py
+++ b/solution.py
@@ -58,7 +58,7 @@
 
     def one(k):
         j = flat[start + k] % maxp
-        e = jnp.where(j * PAGE + pos < length, jnp.exp(scores[k] - top), 0.0)
+        e = jnp.exp(scores[k] - top)
         w = e.astype(jnp.bfloat16)
         return e, jnp.dot(w, page_of(start + k), preferred_element_type=jnp.float32)
 

time: 151 us -> 148 us (0.980); the launches traced: 153 us -> 145 us
  Pallas kernels: 75.3 us -> 62.5 us
  blocking collectives: 33.7 us -> 38.2 us
    pallas_call x1, Pallas kernels: 60.3 us -> 50.8 us  [attend(): pl.pallas_call(pool_kernel, grid_spec=pltpu.PrefetchScalarGridSpec(num_sc...]
    all_gather x1, blocking collectives: 13.4 us -> 17.9 us  [on_device(): mixed_all = lax.all_gather(mixed, 'row', axis=0, tiled=True)]
    pallas_call x1, Pallas kernels: 10.2 us -> 6.84 us  [attend(): pl.pallas_call(land_kernel, grid_spec=pltpu.PrefetchScalarGridSpec(num_sc...]
  transfers between devices with their start and end apart: 2 -> 2, of which waited for: 1 -> 1; matrix products, arithmetic and copies ran while one was open for 9% -> 9% of each run, Pallas kernels for 42% -> 38%
where the time goes in v2:
time: 148 us; the launch traced here: 145 us
  Pallas kernels  62.5 us (42%)
  blocking collectives  38.2 us (26%)
  local copies, waits for them, and re-layouts  20.3 us (14%)
  starting transfers between devices  8.65 us (6%)
  other arithmetic  6.14 us (4%)
  waiting for transfers between devices  5.44 us (4%)
  between operations  2.17 us (1%)
    pallas_call x1, Pallas kernels, attend(): pl.pallas_call(pool_kernel, grid_spec=pltpu.PrefetchScalarGridSpec(num_sc...  50.8 us
    all_gather x1, blocking collectives, on_device(): mixed_all = lax.all_gather(mixed, 'row', axis=0, tiled=True)  17.9 us
    all_gather x1, blocking collectives, on_device(): gathered = lax.all_gather(xn, 'col', axis=0, tiled=True)  10.8 us
    all_to_all x1, blocking collectives, on_device(): lax.all_to_all(partial, 'col', split_axis=0, concat_axis=0, tiled=True)  9.5 us
    pallas_call x1, Pallas kernels, attend(): pl.pallas_call(land_kernel, grid_spec=pltpu.PrefetchScalarGridSpec(num_sc...  6.84 us
    all_to_all x1, waiting for transfers between devices, on_device(): lax.all_to_all(partial, 'row', split_axis=0, concat_axis=0, tiled=True)  5.44 us
    pallas_call x1, Pallas kernels, outgoing_pages(): pl.pallas_call(gather_kernel, grid_spec=pltpu.PrefetchScalarGridSpec(num_...  4.9 us
    all_to_all x1, starting transfers between devices, on_device(): lax.all_to_all(partial, 'row', split_axis=0, concat_axis=0, tiled=True)  4.87 us
  transfers between devices with their start and end apart: 2, of which 1 were waited for; matrix products, arithmetic and copies ran while one was open for 9% of the time, Pallas kernels for 38%

profile of v2, /device:TPU:0, one launch (start us, length us, event | category | flops | bytes accessed | tf_op | source)
XLA Modules:
  0.0 144.9 jit_solution(4780393718424946205)
XLA Ops:
  0.7 0.7 compare_select_fusion.4
  1.4 1.4 scatter_custom_fusion.1
  2.8 1.4 copy.43
  4.3 10.8 %all_gather.6 = bf16[256,512]{1,0:T(8,128)(2,1)S(1)} all-gather(bf16[32,512]{1,0:T(8,128)(2,1)S(1)} %copy-done.4), channel_id=1, replica_groups=mesh['row'=4,'col'=8] {'col'}, dimensions={0}, use_global_device_ids=true | all-gather | bytes 294912 | tf_op jit(solution)/shard_map/all_gather | solution.py:333
  15.1 1.2 gather_fusion.2
  16.2 1.2 convolution_convert_fusion
  17.4 4.9 %all-to-all-start.1 = ((bf16[4,64,768]{2,1,0:T(8,128)(2,1)}), bf16[4,64,768]{2,1,0:T(8,128)(2,1)S(1)}, u32[]{:S(2)}, u32[]{:S(2)}) async-start(bf16[4,64,768]{2,1,0:T(8,128)(2,1)} %bitcast.6), calls=%async_computation.1 | async-start | bytes 786432 | tf_op jit(solution)/shard_map/all_to_all | solution.py:341
  22.5 0.7 select_reduce_fusion
  23.3 0.8 scatter_custom_fusion.2.idx_ref
  24.1 4.9 %shard_map.105 = bf16[40,64,512]{2,1,0:T(8,128)(2,1)} custom-call(s32[40]{0:T(128)S(1)} %scatter_custom_fusion.2.idx_ref, bf16[256,64,512]{2,1,0:T(8,128)(2,1)} %pool_n_ref.1), custom_call_target="tpu_custom_call" | custom-call | tf_op jit(solution)/shard_map/pallas_call | solution.py:278
  29.0 5.4 %all-to-all-done.1 = bf16[4,64,768]{2,1,0:T(8,128)(2,1)S(1)} async-done(((bf16[4,64,768]{2,1,0:T(8,128)(2,1)}), bf16[4,64,768]{2,1,0:T(8,128)(2,1)S(1)}, u32[]{:S(2)}, u32[]{:S(2)}) %all-to-all-start.1) | async-done | bytes 393248 | tf_op jit(solution)/shard_map/all_to_all | solution.py:341
  34.5 3.8 %all-to-all-start.2 = ((bf16[4,10,64,512]{3,2,1,0:T(8,128)(2,1)}), bf16[4,10,64,512]{3,2,1,0:T(8,128)(2,1)S(1)}, u32[]{:S(2)}, u32[]{:S(2)}) async-start(bf16[4,10,64,512]{3,2,1,0:T(8,128)(2,1)} %bitcast.10), calls=%async_computation.2 | async-start | bytes 5242880 | tf_op jit(solution)/shard_map/all_to_all | solution.py:296
  38.3 0.7 gather_fusion.4
  39.0 0.7 gather_fusion.3
  39.7 0.1 multiply_cosine_fusion
  39.8 0.7 tile.8
  40.5 1.7 %copy.44 = f32[64,512]{1,0:T(8,128)} copy(f32[64,512]{0,1:T(8,128)} %bitcast.39) | data formatting | bytes 262144 | tf_op jit(solution)/shard_map/tile | solution.py:350
  42.2 0.7 tile.20
  43.0 1.7 %copy.45 = f32[64,512]{1,0:T(8,128)} copy(f32[64,512]{0,1:T(8,128)} %bitcast.40) | data formatting | bytes 262144 | tf_op jit(solution)/shard_map/tile | solution.py:351
  44.7 0.7 reshape.199.tbl
  45.9 0.6 fusion.26
  47.5 1.1 broadcast_select_fusion.2
  48.7 0.7 reshape.202.qrow_ref
  49.4 0.2 fusion.7
  49.7 0.8 add.114.snew_ref
  50.5 50.8 %shard_map.104 = (f32[64,8,128]{2,1,0:T(8,128)}, f32[64,8,128]{2,1,0:T(8,128)}, f32[64,8,512]{2,1,0:T(8,128)}) custom-call(s32[4096]{0:T(1024)} %reshape.199.tbl, s32[64]{0:T(128)} %lens.3, f32[64,1,512]{2,1,0:T(1,128)} %reshape.202.qrow_ref, f32[64,8,128]{2,1,0:T(8,128)} %add.114.snew_ref, bf16[256,64,512]{2,1,0:T(8,128)(2,1)} %pool_n_ref.1), custom_call_target="tpu_custom_call" | custom-call | tf_op jit(solution)/shard_map/pallas_call | solution.py:203
  101.3 0.5 copy.52
  101.8 3.0 %conditional.1 = (bf16[16,64,512]{2,1,0:T(8,128)(2,1)S(1)}) conditional(s32[]{:T(128)} %clamp.7, (s32[16]{0:T(128)S(1)}, s32[16]{0:T(128)S(1)}, bf16[4,10,64,512]{3,2,1,0:T(8,128)(2,1)S(1)}) %tuple.15, (s32[16]{0:T(128)S(1)}, s32[16]{0:T(128)S(1)}, s32[64]{0:T(128)S(1)}, s32[64]{0:T(128)S(1)}, s32[64]{0:T(128)S(1)}, /*index=5*/s32[64]{0:T(128)S(1)}, ...), branch_computations={%region_8.9_spmd, %region_9.11_spmd} | conditional | flops 2623379 | bytes 17307152 | solution.py:324
  101.8 1.6 %gather_fusion = bf16[16,64,512]{2,1,0:T(8,128)(2,1)} fusion(bf16[40,64,512]{2,1,0:T(8,128)(2,1)S(1)} %bitcast.34, s32[1024]{0:T(1024)S(1)} %pad_clamp_fusion), kind=kCustom, calls=%fused_computation | custom fusion | bytes 2097216 | tf_op jit(solution)/shard_map/cond/branch_0_fun/jit(_take)/gather | solution.py:319
  103.4 1.4 broadcast_select_fusion
  104.8 6.8 %shard_map.106 = (f32[64,8,128]{2,1,0:T(8,128)}, f32[64,8,128]{2,1,0:T(8,128)}, f32[64,8,512]{2,1,0:T(8,128)}) custom-call(s32[4096]{0:T(1024)} %reshape.199.tbl, s32[64]{0:T(128)} %lens.3, f32[64,1,512]{2,1,0:T(1,128)} %reshape.202.qrow_ref, f32[64,8,128]{2,1,0:T(8,128)} %get-tuple-element.45.m_in, f32[64,8,128]{2,1,0:T(8,128)} %get-tuple-element.46.l_in, ...), custom_call_target="tpu_custom_call" | custom-call | tf_op jit(solution)/shard_map/pallas_call | solution.py:217
  111.7 1.4 slice.69
  113.0 0.8 reshape.205
  113.9 0.1 slice_bitcast_fusion.3
  114.0 0.2 pad_maximum_fusion.1
  114.2 0.1 stack.6
  114.4 0.1 copy.55
  114.5 0.1 copy.56
  114.6 0.1 div.52
  114.7 0.1 div.53
  115.0 0.1 copy.54
  115.1 0.1 mul.107
  115.2 0.1 mul.108
  115.4 17.9 %all_gather.7 = bf16[256,256]{1,0:T(8,128)(2,1)S(1)} all-gather(bf16[64,256]{1,0:T(8,128)(2,1)S(1)} %divide_convert_fusion), channel_id=1, replica_groups=mesh['row'=4,'col'=8] {'row'}, dimensions={0}, use_global_device_ids=true | all-gather | bytes 163840 | tf_op jit(solution)/shard_map/all_gather | solution.py:362
  133.3 1.2 gather_fusion.5
  134.5 0.3 convolution_convert_fusion.1
  134.7 9.5 %all_to_all.27 = bf16[8,32,512]{2,1,0:T(8,128)(2,1)S(1)} all-to-all(bf16[8,32,512]{2,1,0:T(8,128)(2,1)S(1)} %bitcast.38), channel_id=1, replica_groups=mesh['row'=4,'col'=8] {'col'}, dimensions={0} | all-to-all | bytes 524288 | tf_op jit(solution)/shard_map/all_to_all | solution.py:368
  144.2 0.7 reduce_sum.56
  (51 shorter events, 1.0 us)
Async XLA Ops:
  0.6 133.8 %copy-start = (bf16[256,512]{1,0:T(8,128)(2,1)S(1)}, bf16[256,512]{1,0:T(8,128)(2,1)}, u32[]{:S(2)}) copy-start(bf16[256,512]{1,0:T(8,128)(2,1)} %param.13) | copy-start | bytes 786436
  0.6 3.7 %copy-start.4 = (bf16[32,512]{1,0:T(8,128)(2,1)S(1)}, bf16[32,512]{1,0:T(8,128)(2,1)}, u32[]{:S(2)}) copy-start(bf16[32,512]{1,0:T(8,128)(2,1)} %param.11) | copy-start | bytes 98308
  15.1 7.2 %copy-start.8 = (s32[64]{0:T(128)S(1)}, s32[64]{0:T(128)}, u32[]{:S(2)}) copy-start(s32[64]{0:T(128)} %param.17) | copy-start | bytes 772
  17.4 17.1 %all-to-all-start.1 = ((bf16[4,64,768]{2,1,0:T(8,128)(2,1)}), bf16[4,64,768]{2,1,0:T(8,128)(2,1)S(1)}, u32[]{:S(2)}, u32[]{:S(2)}) async-start(bf16[4,64,768]{2,1,0:T(8,128)(2,1)} %bitcast.6), calls=%async_computation.1 | async-start | bytes 786432 | tf_op jit(solution)/shard_map/all_to_all | solution.py:341
  34.5 5.2 %copy-start.6 = (s32[64]{0:T(128)S(1)}, s32[64]{0:T(128)}, u32[]{:S(2)}) copy-start(s32[64]{0:T(128)} %lens.3) | copy-start | bytes 772
  34.5 10.2 %copy-start.5 = (s32[64,64]{1,0:T(8,128)S(1)}, s32[64,64]{1,0:T(8,128)}, u32[]{:S(2)}) copy-start(s32[64,64]{1,0:T(8,128)} %param.15) | copy-start | bytes 49156
  34.5 12.8 %copy-start.7 = (s32[256]{0:T(256)S(1)}, s32[256]{0:T(256)}, u32[]{:S(2)}) copy-start(s32[256]{0:T(256)} %param.18) | copy-start | bytes 3076
  34.5 67.3 %all-to-all-start.2 = ((bf16[4,10,64,512]{3,2,1,0:T(8,128)(2,1)}), bf16[4,10,64,512]{3,2,1,0:T(8,128)(2,1)S(1)}, u32[]{:S(2)}, u32[]{:S(2)}) async-start(bf16[4,10,64,512]{3,2,1,0:T(8,128)(2,1)} %bitcast.10), calls=%async_computation.2 | async-start | bytes 5242880 | tf_op jit(solution)/shard_map/all_to_all | solution.py:296
  104.8 6.9 %copy-start.1 = (bf16[16,64,512]{2,1,0:T(8,128)(2,1)}, bf16[16,64,512]{2,1,0:T(8,128)(2,1)S(1)}, u32[]{:S(2)}) copy-start(bf16[16,64,512]{2,1,0:T(8,128)(2,1)S(1)} %get-tuple-element.78.land_ref) | copy-start | bytes 3145732
  111.7 2.6 %copy-start.2 = (f32[64,8,128]{2,1,0:T(8,128)S(1)}, f32[64,8,128]{2,1,0:T(8,128)}, u32[]{:S(2)}) copy-start(f32[64,8,128]{2,1,0:T(8,128)} %get-tuple-element.50) | copy-start | bytes 786436
  111.7 2.6 %copy-start.3 = (f32[64,8,128]{2,1,0:T(8,128)S(1)}, f32[64,8,128]{2,1,0:T(8,128)}, u32[]{:S(2)}) copy-start(f32[64,8,128]{2,1,0:T(8,128)} %get-tuple-element.51) | copy-start | bytes 786436

commit v3 on v0

--- a/solution.py
+++ b/solution.py
@@ -74,8 +74,7 @@
         return total + e0, numer + n0
 
     init = (jnp.zeros((rows, PAGE), jnp.float32), jnp.zeros((rows, lanes), jnp.float32))
-    carry = lax.fori_loop(0, count // 2, two, init)
-    total, numer = lax.fori_loop(count // 2 * 2, count, single, carry)
+    total, numer = lax.fori_loop(0, count, single, init)
     return jnp.sum(total, axis=1, keepdims=True), numer
 
 

time: 151 us -> 165 us (1.093); the launches traced: 153 us -> 164 us
  blocking collectives: 33.7 us -> 61.3 us
  Pallas kernels: 75.3 us -> 58 us
    all_gather x1, blocking collectives: 13.4 us -> 41 us  [on_device(): mixed_all = lax.all_gather(mixed, 'row', axis=0, tiled=True)]
    pallas_call x1, Pallas kernels: 60.3 us -> 46.8 us  [attend(): pl.pallas_call(pool_kernel, grid_spec=pltpu.PrefetchScalarGridSpec(num_sc...]
    pallas_call x1, Pallas kernels: 10.2 us -> 6.47 us  [attend(): pl.pallas_call(land_kernel, grid_spec=pltpu.PrefetchScalarGridSpec(num_sc...]
  transfers between devices with their start and end apart: 2 -> 2, of which waited for: 1 -> 1; matrix products, arithmetic and copies ran while one was open for 9% -> 8% of each run, Pallas kernels for 42% -> 31%
where the time goes in v3:
time: 165 us; the launch traced here: 164 us
  blocking collectives  61.3 us (37%)
  Pallas kernels  58 us (35%)
  local copies, waits for them, and re-layouts  20.3 us (12%)
  starting transfers between devices  8.65 us (5%)
  other arithmetic  6.14 us (4%)
  waiting for transfers between devices  5.67 us (3%)
  between operations  2.17 us (1%)
    pallas_call x1, Pallas kernels, attend(): pl.pallas_call(pool_kernel, grid_spec=pltpu.PrefetchScalarGridSpec(num_sc...  46.8 us
    all_gather x1, blocking collectives, on_device(): mixed_all = lax.all_gather(mixed, 'row', axis=0, tiled=True)  41 us
    all_gather x1, blocking collectives, on_device(): gathered = lax.all_gather(xn, 'col', axis=0, tiled=True)  10.8 us
    all_to_all x1, blocking collectives, on_device(): lax.all_to_all(partial, 'col', split_axis=0, concat_axis=0, tiled=True)  9.5 us
    pallas_call x1, Pallas kernels, attend(): pl.pallas_call(land_kernel, grid_spec=pltpu.PrefetchScalarGridSpec(num_sc...  6.47 us
    all_to_all x1, waiting for transfers between devices, on_device(): lax.all_to_all(partial, 'row', split_axis=0, concat_axis=0, tiled=True)  5.66 us
    all_to_all x1, starting transfers between devices, on_device(): lax.all_to_all(partial, 'row', split_axis=0, concat_axis=0, tiled=True)  4.87 us
    pallas_call x1, Pallas kernels, outgoing_pages(): pl.pallas_call(gather_kernel, grid_spec=pltpu.PrefetchScalarGridSpec(num_...  4.68 us
  transfers between devices with their start and end apart: 2, of which 1 were waited for; matrix products, arithmetic and copies ran while one was open for 8% of the time, Pallas kernels for 31%

profile of v3, /device:TPU:0, one launch (start us, length us, event | category | flops | bytes accessed | tf_op | source)
XLA Modules:
  0.0 163.6 jit_solution(9460181793949631238)
XLA Ops:
  0.7 0.7 compare_select_fusion.4
  1.4 1.4 scatter_custom_fusion.1
  2.8 1.4 copy.43
  4.3 10.8 %all_gather.6 = bf16[256,512]{1,0:T(8,128)(2,1)S(1)} all-gather(bf16[32,512]{1,0:T(8,128)(2,1)S(1)} %copy-done.4), channel_id=1, replica_groups=mesh['row'=4,'col'=8] {'col'}, dimensions={0}, use_global_device_ids=true | all-gather | bytes 294912 | tf_op jit(solution)/shard_map/all_gather | solution.py:332
  15.1 1.2 gather_fusion.2
  16.2 1.2 convolution_convert_fusion
  17.4 4.9 %all-to-all-start.1 = ((bf16[4,64,768]{2,1,0:T(8,128)(2,1)}), bf16[4,64,768]{2,1,0:T(8,128)(2,1)S(1)}, u32[]{:S(2)}, u32[]{:S(2)}) async-start(bf16[4,64,768]{2,1,0:T(8,128)(2,1)} %bitcast.6), calls=%async_computation.1 | async-start | bytes 786432 | tf_op jit(solution)/shard_map/all_to_all | solution.py:340
  22.5 0.7 select_reduce_fusion
  23.3 0.8 scatter_custom_fusion.2.idx_ref
  24.1 4.7 %shard_map.105 = bf16[40,64,512]{2,1,0:T(8,128)(2,1)} custom-call(s32[40]{0:T(128)S(1)} %scatter_custom_fusion.2.idx_ref, bf16[256,64,512]{2,1,0:T(8,128)(2,1)} %pool_n_ref.1), custom_call_target="tpu_custom_call" | custom-call | tf_op jit(solution)/shard_map/pallas_call | solution.py:277
  28.8 5.7 %all-to-all-done.1 = bf16[4,64,768]{2,1,0:T(8,128)(2,1)S(1)} async-done(((bf16[4,64,768]{2,1,0:T(8,128)(2,1)}), bf16[4,64,768]{2,1,0:T(8,128)(2,1)S(1)}, u32[]{:S(2)}, u32[]{:S(2)}) %all-to-all-start.1) | async-done | bytes 393248 | tf_op jit(solution)/shard_map/all_to_all | solution.py:340
  34.5 3.8 %all-to-all-start.2 = ((bf16[4,10,64,512]{3,2,1,0:T(8,128)(2,1)}), bf16[4,10,64,512]{3,2,1,0:T(8,128)(2,1)S(1)}, u32[]{:S(2)}, u32[]{:S(2)}) async-start(bf16[4,10,64,512]{3,2,1,0:T(8,128)(2,1)} %bitcast.10), calls=%async_computation.2 | async-start | bytes 5242880 | tf_op jit(solution)/shard_map/all_to_all | solution.py:295
  38.3 0.7 gather_fusion.4
  39.0 0.7 gather_fusion.3
  39.7 0.1 multiply_cosine_fusion
  39.8 0.7 tile.8
  40.5 1.7 %copy.44 = f32[64,512]{1,0:T(8,128)} copy(f32[64,512]{0,1:T(8,128)} %bitcast.39) | data formatting | bytes 262144 | tf_op jit(solution)/shard_map/tile | solution.py:349
  42.2 0.7 tile.20
  43.0 1.7 %copy.45 = f32[64,512]{1,0:T(8,128)} copy(f32[64,512]{0,1:T(8,128)} %bitcast.40) | data formatting | bytes 262144 | tf_op jit(solution)/shard_map/tile | solution.py:350
  44.7 0.7 reshape.199.tbl
  45.9 0.6 fusion.26
  47.5 1.1 broadcast_select_fusion.2
  48.7 0.7 reshape.202.qrow_ref
  49.4 0.2 fusion.7
  49.7 0.8 add.114.snew_ref
  50.5 46.8 %shard_map.104 = (f32[64,8,128]{2,1,0:T(8,128)}, f32[64,8,128]{2,1,0:T(8,128)}, f32[64,8,512]{2,1,0:T(8,128)}) custom-call(s32[4096]{0:T(1024)} %reshape.199.tbl, s32[64]{0:T(128)} %lens.3, f32[64,1,512]{2,1,0:T(1,128)} %reshape.202.qrow_ref, f32[64,8,128]{2,1,0:T(8,128)} %add.114.snew_ref, bf16[256,64,512]{2,1,0:T(8,128)(2,1)} %pool_n_ref.1), custom_call_target="tpu_custom_call" | custom-call | tf_op jit(solution)/shard_map/pallas_call | solution.py:202
  97.3 0.5 copy.52
  97.8 3.0 %conditional.1 = (bf16[16,64,512]{2,1,0:T(8,128)(2,1)S(1)}) conditional(s32[]{:T(128)} %clamp.7, (s32[16]{0:T(128)S(1)}, s32[16]{0:T(128)S(1)}, bf16[4,10,64,512]{3,2,1,0:T(8,128)(2,1)S(1)}) %tuple.15, (s32[16]{0:T(128)S(1)}, s32[16]{0:T(128)S(1)}, s32[64]{0:T(128)S(1)}, s32[64]{0:T(128)S(1)}, s32[64]{0:T(128)S(1)}, /*index=5*/s32[64]{0:T(128)S(1)}, ...), branch_computations={%region_8.9_spmd, %region_9.11_spmd} | conditional | flops 2623379 | bytes 17307152 | solution.py:323
  97.9 1.6 gather_fusion
  99.4 1.4 broadcast_select_fusion
  100.8 6.5 %shard_map.106 = (f32[64,8,128]{2,1,0:T(8,128)}, f32[64,8,128]{2,1,0:T(8,128)}, f32[64,8,512]{2,1,0:T(8,128)}) custom-call(s32[4096]{0:T(1024)} %reshape.199.tbl, s32[64]{0:T(128)} %lens.3, f32[64,1,512]{2,1,0:T(1,128)} %reshape.202.qrow_ref, f32[64,8,128]{2,1,0:T(8,128)} %get-tuple-element.45.m_in, f32[64,8,128]{2,1,0:T(8,128)} %get-tuple-element.46.l_in, ...), custom_call_target="tpu_custom_call" | custom-call | tf_op jit(solution)/shard_map/pallas_call | solution.py:216
  107.3 1.4 slice.69
  108.7 0.8 reshape.205
  109.5 0.1 slice_bitcast_fusion.3
  109.6 0.2 pad_maximum_fusion.1
  109.8 0.1 stack.6
  110.0 0.1 copy.55
  110.1 0.1 copy.56
  110.2 0.1 div.52
  110.4 0.1 div.53
  110.6 0.1 copy.54
  110.7 0.1 mul.107
  110.9 0.1 mul.108
  111.0 41.0 %all_gather.7 = bf16[256,256]{1,0:T(8,128)(2,1)S(1)} all-gather(bf16[64,256]{1,0:T(8,128)(2,1)S(1)} %divide_convert_fusion), channel_id=1, replica_groups=mesh['row'=4,'col'=8] {'row'}, dimensions={0}, use_global_device_ids=true | all-gather | bytes 163840 | tf_op jit(solution)/shard_map/all_gather | solution.py:361
  152.0 1.2 gather_fusion.5
  153.2 0.3 convolution_convert_fusion.1
  153.5 9.5 %all_to_all.27 = bf16[8,32,512]{2,1,0:T(8,128)(2,1)S(1)} all-to-all(bf16[8,32,512]{2,1,0:T(8,128)(2,1)S(1)} %bitcast.38), channel_id=1, replica_groups=mesh['row'=4,'col'=8] {'col'}, dimensions={0} | all-to-all | bytes 524288 | tf_op jit(solution)/shard_map/all_to_all | solution.py:367
  163.0 0.7 reduce_sum.56
  (51 shorter events, 1.0 us)
Async XLA Ops:
  0.6 152.5 %copy-start = (bf16[256,512]{1,0:T(8,128)(2,1)S(1)}, bf16[256,512]{1,0:T(8,128)(2,1)}, u32[]{:S(2)}) copy-start(bf16[256,512]{1,0:T(8,128)(2,1)} %param.13) | copy-start | bytes 786436
  0.6 3.7 %copy-start.4 = (bf16[32,512]{1,0:T(8,128)(2,1)S(1)}, bf16[32,512]{1,0:T(8,128)(2,1)}, u32[]{:S(2)}) copy-start(bf16[32,512]{1,0:T(8,128)(2,1)} %param.11) | copy-start | bytes 98308
  15.1 7.2 %copy-start.8 = (s32[64]{0:T(128)S(1)}, s32[64]{0:T(128)}, u32[]{:S(2)}) copy-start(s32[64]{0:T(128)} %param.17) | copy-start | bytes 772
  17.4 17.1 %all-to-all-start.1 = ((bf16[4,64,768]{2,1,0:T(8,128)(2,1)}), bf16[4,64,768]{2,1,0:T(8,128)(2,1)S(1)}, u32[]{:S(2)}, u32[]{:S(2)}) async-start(bf16[4,64,768]{2,1,0:T(8,128)(2,1)} %bitcast.6), calls=%async_computation.1 | async-start | bytes 786432 | tf_op jit(solution)/shard_map/all_to_all | solution.py:340
  34.5 5.2 %copy-start.6 = (s32[64]{0:T(128)S(1)}, s32[64]{0:T(128)}, u32[]{:S(2)}) copy-start(s32[64]{0:T(128)} %lens.3) | copy-start | bytes 772
  34.5 10.2 %copy-start.5 = (s32[64,64]{1,0:T(8,128)S(1)}, s32[64,64]{1,0:T(8,128)}, u32[]{:S(2)}) copy-start(s32[64,64]{1,0:T(8,128)} %param.15) | copy-start | bytes 49156
  34.5 12.8 %copy-start.7 = (s32[256]{0:T(256)S(1)}, s32[256]{0:T(256)}, u32[]{:S(2)}) copy-start(s32[256]{0:T(256)} %param.18) | copy-start | bytes 3076
  34.5 63.3 %all-to-all-start.2 = ((bf16[4,10,64,512]{3,2,1,0:T(8,128)(2,1)}), bf16[4,10,64,512]{3,2,1,0:T(8,128)(2,1)S(1)}, u32[]{:S(2)}, u32[]{:S(2)}) async-start(bf16[4,10,64,512]{3,2,1,0:T(8,128)(2,1)} %bitcast.10), calls=%async_computation.2 | async-start | bytes 5242880 | tf_op jit(solution)/shard_map/all_to_all | solution.py:295
  100.8 6.5 %copy-start.1 = (bf16[16,64,512]{2,1,0:T(8,128)(2,1)}, bf16[16,64,512]{2,1,0:T(8,128)(2,1)S(1)}, u32[]{:S(2)}) copy-start(bf16[16,64,512]{2,1,0:T(8,128)(2,1)S(1)} %get-tuple-element.78.land_ref) | copy-start | bytes 3145732
  107.3 2.6 %copy-start.2 = (f32[64,8,128]{2,1,0:T(8,128)S(1)}, f32[64,8,128]{2,1,0:T(8,128)}, u32[]{:S(2)}) copy-start(f32[64,8,128]{2,1,0:T(8,128)} %get-tuple-element.50) | copy-start | bytes 786436
  107.3 2.6 %copy-start.3 = (f32[64,8,128]{2,1,0:T(8,128)S(1)}, f32[64,8,128]{2,1,0:T(8,128)}, u32[]{:S(2)}) copy-start(f32[64,8,128]{2,1,0:T(8,128)} %get-tuple-element.51) | copy-start | bytes 786436
